TPU v7x, 32 devices: a whole 2x2x4 slice. The times are simulated.
32 devices in a mesh: groups: 2 (over y), pix: 4 (over z), sub: 2 (over x), inner: 2 (over core).
Axes of the slice: x: 2, y: 2, z: 4, core: 2. Of those that a mesh axis runs over, the one named last changes fastest.
Arguments:
- cube: bfloat16 [20480, 256], P(('groups', 'pix', 'sub', 'inner')), parts along dimension 0, may hold values from -70 to 70
Outputs:
- spectra: bfloat16 [256, 16, 1280], P(('pix', 'sub'), 'groups', 'inner'), parts along dimension 1
There are 2 independent parts, one for each index of `groups`. A program takes and returns all parts, laid end to end along the dimension named above; each array names one. Nothing has to cross between parts.
All inputs are finite; a program needn't handle non-finite values.
Results may differ from a plain program's by a relative error of at most 0.0067.
Values may be sent and summed in bfloat16 or wider, within the bound.
No kernel may reach another device: no remote copies, remote signals or barrier semaphores. Data moves between devices by JAX's collectives and lax.ppermute only.
A program may use at most 64 MiB of HBM per device.

v0:
```python
import math
import jax
import jax.numpy as jnp
from jax import lax
from jax.sharding import PartitionSpec as P

MODES = 32
ITERS = 4


def matmul_high(left, right):
    return jnp.dot(left, right, precision=lax.Precision.HIGHEST)


def leading_modes(gram_matrix, width_count, sweeps):
    mode_basis = jnp.eye(gram_matrix.shape[0], width_count, dtype=jnp.float32)
    for iteration in range(sweeps):
        product = matmul_high(gram_matrix, mode_basis)
        cross_gram = matmul_high(product.T, product)
        lower_factor = jnp.linalg.cholesky(cross_gram)
        mode_basis = jax.scipy.linalg.solve_triangular(lower_factor, product.T, lower=True).T
    return mode_basis


def delay_table(channels):
    middle = channels // 2
    row_index = lax.broadcasted_iota(jnp.int32, (channels, channels), 0)
    col_index = lax.broadcasted_iota(jnp.int32, (channels, channels), 1)
    harmonic = jnp.where(row_index <= middle, row_index, row_index - middle)
    angles = (harmonic * col_index % channels).astype(jnp.float32) * (2.0 * math.pi / channels)
    values = jnp.where(row_index <= middle, jnp.cos(angles), jnp.sin(angles)) / math.sqrt(channels)
    return values.astype(jnp.bfloat16)


def local(cube):
    pixels, channels = cube.shape
    pixel_count = pixels * lax.axis_size(("pix", "sub", "inner"))
    partial_gram = lax.dot_general(
        cube, cube, (((0,), (0,)), ((), ())), preferred_element_type=jnp.float32
    )
    gram_matrix = lax.psum(partial_gram, ("pix", "sub", "inner"))
    gram_matrix = gram_matrix / pixel_count
    mode_basis = leading_modes(gram_matrix, MODES, ITERS)
    modes_b = mode_basis.astype(jnp.bfloat16)
    amplitudes = jnp.dot(cube, modes_b, preferred_element_type=jnp.float32).astype(jnp.bfloat16)
    cleaned = (cube - jnp.dot(amplitudes, modes_b.T, preferred_element_type=jnp.float32)).astype(
        jnp.bfloat16
    )
    table_b = delay_table(channels)
    coefficients = lax.dot_general(
        table_b, cleaned, (((1,), (1,)), ((), ())), preferred_element_type=jnp.float32
    ).astype(jnp.bfloat16)
    spectra = lax.all_to_all(
        coefficients[:, None, :], ("pix", "sub"), split_axis=0, concat_axis=1, tiled=True
    )
    return spectra


def solution(mesh):
    return jax.shard_map(
        local,
        mesh=mesh,
        in_specs=(P(("groups", "pix", "sub", "inner"), None),),
        out_specs=P(("pix", "sub"), "groups", "inner"),
        check_vma=False,
    )
```

profile of v0, /device:TPU:0, one launch (start us, length us, event | category | flops | bytes accessed | tf_op | source)
XLA Modules:
  0.0 160.6 jit_solution(15145366954899768476)
XLA Ops:
  6.5 2.1 %fusion.59 = f32[256,256]{1,0:T(8,128)} fusion(bf16[640,256]{1,0:T(8,128)(2,1)} %param.4), kind=kOutput, calls=%fused_computation.85 | convolution fusion | flops 83886080 | bytes 589824 | tf_op jit(solution)/shard_map/dot_general | solution.py:38
  8.7 94.6 %all-reduce.2.cloned.1.call-done = f32[256,256]{1,0:T(8,128)} async-done(((f32[256,256]{1,0:T(8,128)}), f32[256,256]{1,0:T(8,128)}) %all-reduce.2.cloned.1.call-update) | async-done | bytes 262160 | tf_op jit(solution)/shard_map/psum | solution.py:41
  103.3 1.3 fusion.12
  104.8 2.9 %cholesky.74 = f32[32,32]{1,0:T(8,128)S(1)} custom-call(f32[32,32]{1,0:T(8,128)S(1)} %fusion.43), custom_call_target="Cholesky" | custom-call | tf_op jit(solution)/shard_map/jit(cholesky)/cholesky | solution.py:20
  107.8 0.6 compare_reduce_fusion.3
  108.4 0.7 fusion.32
  109.1 2.4 %custom-call.8 = f32[1,32,32]{1,2,0:T(8,128)S(1)} custom-call(f32[1,32,32]{2,1,0:T(8,128)S(1)} %fusion.32), custom_call_target="InvertDiagBlocksLowerTriangular" | custom-call | tf_op jit(solution)/shard_map/jit(_solve_triangular)/triangular_solve | solution.py:21
  111.5 0.2 fusion.30
  111.8 0.3 fusion.10
  112.4 2.9 %cholesky.85 = f32[32,32]{1,0:T(8,128)S(1)} custom-call(f32[32,32]{1,0:T(8,128)S(1)} %fusion.41), custom_call_target="Cholesky" | custom-call | tf_op jit(solution)/shard_map/jit(cholesky)/cholesky | solution.py:20
  115.3 0.6 compare_reduce_fusion.2
  116.0 0.7 fusion.33
  116.6 2.4 %custom-call.9 = f32[1,32,32]{1,2,0:T(8,128)S(1)} custom-call(f32[1,32,32]{2,1,0:T(8,128)S(1)} %fusion.33), custom_call_target="InvertDiagBlocksLowerTriangular" | custom-call | tf_op jit(solution)/shard_map/jit(_solve_triangular)/triangular_solve | solution.py:21
  119.1 0.2 fusion.28
  119.3 0.3 fusion.8
  119.9 2.9 %cholesky.96 = f32[32,32]{1,0:T(8,128)S(1)} custom-call(f32[32,32]{1,0:T(8,128)S(1)} %fusion.39), custom_call_target="Cholesky" | custom-call | tf_op jit(solution)/shard_map/jit(cholesky)/cholesky | solution.py:20
  122.9 0.6 compare_reduce_fusion.1
  123.5 0.7 fusion.34
  124.2 2.4 %custom-call.10 = f32[1,32,32]{1,2,0:T(8,128)S(1)} custom-call(f32[1,32,32]{2,1,0:T(8,128)S(1)} %fusion.34), custom_call_target="InvertDiagBlocksLowerTriangular" | custom-call | tf_op jit(solution)/shard_map/jit(_solve_triangular)/triangular_solve | solution.py:21
  126.6 0.2 fusion.26
  126.9 0.3 fusion.6
  127.5 2.9 %cholesky.107 = f32[32,32]{1,0:T(8,128)S(1)} custom-call(f32[32,32]{1,0:T(8,128)S(1)} %fusion.37), custom_call_target="Cholesky" | custom-call | tf_op jit(solution)/shard_map/jit(cholesky)/cholesky | solution.py:20
  130.4 0.6 compare_reduce_fusion
  131.1 0.7 fusion.35
  131.7 2.4 %custom-call.11 = f32[1,32,32]{1,2,0:T(8,128)S(1)} custom-call(f32[1,32,32]{2,1,0:T(8,128)S(1)} %fusion.35), custom_call_target="InvertDiagBlocksLowerTriangular" | custom-call | tf_op jit(solution)/shard_map/jit(_solve_triangular)/triangular_solve | solution.py:21
  134.2 0.2 convolution_convert_fusion.2
  134.6 1.5 fusion.1
  136.1 0.5 broadcast.63
  136.6 0.8 reduce.4
  137.6 15.0 %all_to_all.18 = bf16[8,2,10240]{2,1,0:T(2,128)(2,1)S(1)} all-to-all(bf16[8,2,10240]{2,1,0:T(2,128)(2,1)S(1)} %reshape.8), channel_id=1, replica_groups=mesh['groups'=2,'pix'=4,'sub'=2,'inner'=2] {'pix','sub'}, dimensions={0} | all-to-all | bytes 655360 | tf_op jit(solution)/shard_map/all_to_all | solution.py:53
  152.5 0.3 reshape.9
  152.9 0.8 copy.18
  (27 shorter events, 1.4 us)
Async XLA Ops:
  6.5 96.7 %all-reduce.2.cloned.1.call-start = ((), (), s32[]{:S(2)}) async-start(), calls=%async_computation.1 | async-start | bytes 524288 | tf_op jit(solution)/shard_map/psum | solution.py:41
  103.3 8.5 %copy-start = (f32[256,256]{1,0:T(8,128)S(1)}, f32[256,256]{1,0:T(8,128)}, u32[]{:S(2)}) copy-start(f32[256,256]{1,0:T(8,128)} %all-reduce.2.cloned.1.call-done) | copy-start | bytes 786436
  126.6 7.8 %copy-start.1 = (bf16[640,256]{1,0:T(8,128)(2,1)S(1)}, bf16[640,256]{1,0:T(8,128)(2,1)}, u32[]{:S(2)}) copy-start(bf16[640,256]{1,0:T(8,128)(2,1)} %param.4) | copy-start | bytes 983044
Sparse Core Ops, SparseCore 0:
  10.7 92.4 all-reduce.1
where the time goes:
time: 161 us
  waiting for transfers between devices  94.6 us (59%)
  other arithmetic  27.6 us (17%)
  blocking collectives  15 us (9%)
  between operations  13.6 us (8%)
  matrix products  7.73 us (5%)
  local copies, waits for them, and re-layouts  2.08 us (1%)
    psum x1, waiting for transfers between devices, local(): gram_matrix = lax.psum(partial_gram, ('pix', 'sub', 'inner'))  94.6 us
    all_to_all x1, blocking collectives, local(): lax.all_to_all(coefficients[:, None, :], ('pix', 'sub'), split_axis=0, co...  15 us
    another operation x12, other arithmetic, leading_modes(): lower_factor = jnp.linalg.cholesky(cross_gram)  14.4 us
    another operation x8, other arithmetic, leading_modes(): jax.scipy.linalg.solve_triangular(lower_factor, product.T, lower=True)  12.3 us
  transfers between devices with their start and end apart: 1, of which 1 were waited for; matrix products, arithmetic and copies ran while one was open for 0% of the time, Pallas kernels for 0%

commit v1 on v0

--- a/solution.py
+++ b/solution.py
@@ -38,7 +38,10 @@
     partial_gram = lax.dot_general(
         cube, cube, (((0,), (0,)), ((), ())), preferred_element_type=jnp.float32
     )
-    gram_matrix = lax.psum(partial_gram, ("pix", "sub", "inner"))
+    _part_frame = lambda local_values: lax.all_gather(local_values, ("pix", "sub", "inner")).sum(
+        axis=0
+    )
+    gram_matrix = _part_frame(partial_gram)
     gram_matrix = gram_matrix / pixel_count
     mode_basis = leading_modes(gram_matrix, MODES, ITERS)
     modes_b = mode_basis.astype(jnp.bfloat16)

time: 161 us -> 121 us (0.75)
  waiting for transfers between devices: 94.6 us -> 53.9 us
  other arithmetic: 27.6 us -> 30.1 us
    psum x1 -> x0, waiting for transfers between devices: 94.6 us -> none  [local(): gram_matrix = lax.psum(partial_gram, ('pix', 'sub', 'inner'))]
    all_gather x0 -> x1, waiting for transfers between devices: none -> 53.9 us  [local(): lax.all_gather(local_values, ('pix', 'sub', 'inner')).sum(axis=0)]
    reduce_sum x0 -> x1, other arithmetic: none -> 2.48 us  [local(): lax.all_gather(local_values, ('pix', 'sub', 'inner')).sum(axis=0)]
where the time goes in v1:
time: 121 us
  waiting for transfers between devices  53.9 us (45%)
  other arithmetic  30.1 us (25%)
  blocking collectives  14.3 us (12%)
  between operations  13.6 us (11%)
  matrix products  6.76 us (6%)
  local copies, waits for them, and re-layouts  2.07 us (2%)
    all_gather x1, waiting for transfers between devices, local(): lax.all_gather(local_values, ('pix', 'sub', 'inner')).sum(axis=0)  53.9 us
    another operation x12, other arithmetic, leading_modes(): lower_factor = jnp.linalg.cholesky(cross_gram)  14.4 us
    all_to_all x1, blocking collectives, local(): lax.all_to_all(coefficients[:, None, :], ('pix', 'sub'), split_axis=0, co...  14.3 us
    another operation x8, other arithmetic, leading_modes(): jax.scipy.linalg.solve_triangular(lower_factor, product.T, lower=True)  12.3 us
    reduce_sum x1, other arithmetic, local(): lax.all_gather(local_values, ('pix', 'sub', 'inner')).sum(axis=0)  2.48 us
  transfers between devices with their start and end apart: 1, of which 1 were waited for; matrix products, arithmetic and copies ran while one was open for 0% of the time, Pallas kernels for 0%

profile of v1, /device:TPU:0, one launch (start us, length us, event | category | flops | bytes accessed | tf_op | source)
XLA Modules:
  0.0 120.7 jit_solution(13079681372410257915)
XLA Ops:
  6.5 2.1 %fusion.59 = f32[256,256]{1,0:T(8,128)} fusion(bf16[640,256]{1,0:T(8,128)(2,1)} %param.4), kind=kOutput, calls=%fused_computation.85 | convolution fusion | flops 83886080 | bytes 589824 | tf_op jit(solution)/shard_map/dot_general | solution.py:38
  8.7 53.9 %all-gather.3.cloned.1.call-done = f32[4096,256]{1,0:T(8,128)} async-done(((f32[256,256]{1,0:T(8,128)}), f32[4096,256]{1,0:T(8,128)}) %all-gather.3.cloned.1.call-update) | async-done | bytes 4194320 | tf_op jit(solution)/shard_map/all_gather | solution.py:41
  62.6 2.5 %reduce_sum.9 = f32[256,256]{1,0:T(8,128)S(1)} reduce(f32[16,256,256]{2,1,0:T(8,128)} %bitcast.73, f32[]{:T(128)} %constant.58.clone.1), dimensions={0}, to_apply=%region_0.0 | reduce | flops 983040 | bytes 4456452 | tf_op jit(solution)/shard_map/reduce_sum | solution.py:41
  65.1 0.3 fusion.12
  65.6 2.9 %cholesky.74 = f32[32,32]{1,0:T(8,128)S(1)} custom-call(f32[32,32]{1,0:T(8,128)S(1)} %fusion.43), custom_call_target="Cholesky" | custom-call | tf_op jit(solution)/shard_map/jit(cholesky)/cholesky | solution.py:20
  68.6 0.6 compare_reduce_fusion.3
  69.2 0.7 fusion.32
  69.9 2.4 %custom-call.8 = f32[1,32,32]{1,2,0:T(8,128)S(1)} custom-call(f32[1,32,32]{2,1,0:T(8,128)S(1)} %fusion.32), custom_call_target="InvertDiagBlocksLowerTriangular" | custom-call | tf_op jit(solution)/shard_map/jit(_solve_triangular)/triangular_solve | solution.py:21
  72.3 0.2 fusion.30
  72.6 0.3 fusion.10
  73.2 2.9 %cholesky.85 = f32[32,32]{1,0:T(8,128)S(1)} custom-call(f32[32,32]{1,0:T(8,128)S(1)} %fusion.41), custom_call_target="Cholesky" | custom-call | tf_op jit(solution)/shard_map/jit(cholesky)/cholesky | solution.py:20
  76.1 0.6 compare_reduce_fusion.2
  76.8 0.7 fusion.33
  77.4 2.4 %custom-call.9 = f32[1,32,32]{1,2,0:T(8,128)S(1)} custom-call(f32[1,32,32]{2,1,0:T(8,128)S(1)} %fusion.33), custom_call_target="InvertDiagBlocksLowerTriangular" | custom-call | tf_op jit(solution)/shard_map/jit(_solve_triangular)/triangular_solve | solution.py:21
  79.9 0.2 fusion.28
  80.1 0.3 fusion.8
  80.7 2.9 %cholesky.96 = f32[32,32]{1,0:T(8,128)S(1)} custom-call(f32[32,32]{1,0:T(8,128)S(1)} %fusion.39), custom_call_target="Cholesky" | custom-call | tf_op jit(solution)/shard_map/jit(cholesky)/cholesky | solution.py:20
  83.7 0.6 compare_reduce_fusion.1
  84.3 0.7 fusion.34
  85.0 2.4 %custom-call.10 = f32[1,32,32]{1,2,0:T(8,128)S(1)} custom-call(f32[1,32,32]{2,1,0:T(8,128)S(1)} %fusion.34), custom_call_target="InvertDiagBlocksLowerTriangular" | custom-call | tf_op jit(solution)/shard_map/jit(_solve_triangular)/triangular_solve | solution.py:21
  87.7 0.3 fusion.6
  88.3 2.9 %cholesky.107 = f32[32,32]{1,0:T(8,128)S(1)} custom-call(f32[32,32]{1,0:T(8,128)S(1)} %fusion.37), custom_call_target="Cholesky" | custom-call | tf_op jit(solution)/shard_map/jit(cholesky)/cholesky | solution.py:20
  91.2 0.6 compare_reduce_fusion
  91.9 0.7 fusion.35
  92.5 2.4 %custom-call.11 = f32[1,32,32]{1,2,0:T(8,128)S(1)} custom-call(f32[1,32,32]{2,1,0:T(8,128)S(1)} %fusion.35), custom_call_target="InvertDiagBlocksLowerTriangular" | custom-call | tf_op jit(solution)/shard_map/jit(_solve_triangular)/triangular_solve | solution.py:21
  95.0 0.2 convolution_convert_fusion.2
  95.4 1.5 %fusion.1 = bf16[256,1,640]{2,0,1:T(8,128)(2,1)S(1)} fusion(bf16[32,640]{1,0:T(8,128)(2,1)S(1)} %convolution_convert_fusion.1, bf16[32,256]{1,0:T(8,128)(2,1)S(1)} %convolution_convert_fusion.2, bf16[640,256]{1,0:T(8,128)(2,1)S(1)} %copy-done, s32[256]{0:T(256)S(1)} %iota_add_fusion, pred[256]{0:T(512)(128)(4,1)S(1)} %iota_compare_fusion.4), kind=kOutput, calls=%fused_computation.3 | convolution fusion | flops 96206848 | bytes 713984 | tf_op jit(solution)/shard_map/dot_general | solution.py:53
  96.9 0.5 broadcast.63
  97.4 0.8 reduce.4
  98.4 14.3 %all_to_all.18 = bf16[8,2,10240]{2,1,0:T(2,128)(2,1)S(1)} all-to-all(bf16[8,2,10240]{2,1,0:T(2,128)(2,1)S(1)} %reshape.9), channel_id=1, replica_groups=mesh['groups'=2,'pix'=4,'sub'=2,'inner'=2] {'pix','sub'}, dimensions={0} | all-to-all | bytes 655360 | tf_op jit(solution)/shard_map/all_to_all | solution.py:56
  112.6 0.3 reshape.10
  113.0 0.8 copy.18
  (26 shorter events, 1.7 us)
Async XLA Ops:
  6.5 88.7 %copy-start = (bf16[640,256]{1,0:T(8,128)(2,1)S(1)}, bf16[640,256]{1,0:T(8,128)(2,1)}, u32[]{:S(2)}) copy-start(bf16[640,256]{1,0:T(8,128)(2,1)} %param.4) | copy-start | bytes 983044
  6.5 56.1 %all-gather.3.cloned.1.call-start = ((), (), s32[]{:S(2)}) async-start(), calls=%async_computation.1 | async-start | bytes 4456448 | tf_op jit(solution)/shard_map/all_gather | solution.py:41
Sparse Core Ops, SparseCore 0:
  9.5 53.0 all-gather.2
